TPU v7x, 128 devices: a whole 4x4x4 slice. The times are simulated.
128 devices in a mesh: req: 8 (over x, core), kv: 16 (over y, z).
Axes of the slice: x: 4, y: 4, z: 4, core: 2. Of those that a mesh axis runs over, the one named last changes fastest.
Arguments:
- x_steps: bfloat16 [4, 1024, 1536], P(None, ('req', 'kv')), may hold values from -6 to 6
- lengths: int32 [128], replicated, may hold values from 16 to 8192
- perm: int32 [128], replicated, may hold values from 0 to 127, as said below
- parents: int32 [4, 1024], replicated, may hold values from 0 to 7
- table: int32 [1024, 9], P(('req', 'kv')), may hold values from 0 to 9215, as said below
- pool: bfloat16 [9216, 128, 256], P(('req', 'kv')), may hold values from -900 to 900
- norm_attn: float32 [1536], replicated, may hold values from 0.1 to 1.9
- w_query: bfloat16 [1536, 1536], replicated, may hold values from -0.15625 to 0.15625
- w_keyval: bfloat16 [1536, 256], replicated, may hold values from -0.15625 to 0.15625
- w_out: bfloat16 [1536, 1536], replicated, may hold values from -0.15625 to 0.15625
- norm_mlp: float32 [1536], replicated, may hold values from 0.1 to 1.9
- w_gate: bfloat16 [1536, 4608], P(None, 'kv'), may hold values from -0.15625 to 0.15625
- w_up: bfloat16 [1536, 4608], P(None, 'kv'), may hold values from -0.15625 to 0.15625
- w_down: bfloat16 [4608, 1536], P('kv'), may hold values from -0.09375 to 0.09375
Outputs:
- outputs: bfloat16 [4, 1024, 1536], P(None, ('req', 'kv'))
Inputs may be any that keep to these rules, and one draw needn't show every extreme that they name: perm is a permutation with perm[s] % 16 == s % 16; among the 8 slots s with one s // 16 and one s % 16 // 8, every req index occurs as perm[s] // 16 exactly once. The entries of row b lie in [(b // 8) * 72, (b // 8 + 1) * 72); no page appears twice in the table.
All inputs are finite; a program needn't handle non-finite values.
Results may differ from a plain program's by a relative error of at most 0.02.
Values may be sent and summed in bfloat16 or wider, within the bound.
No kernel may reach another device: no remote copies, remote signals or barrier semaphores. Data moves between devices by JAX's collectives and lax.ppermute only.
A program may use at most 192 MiB of HBM per device.

v0:
```python
import jax
import jax.numpy as jnp
from jax import lax
from jax.sharding import PartitionSpec as P

WINDOW = 1024
PAGE = 128
BEAMS = 8
EPSILON = 1e-06
NEGATIVE = -1e30


def merged_2(array, axis, combine):
    everything = jax.tree.map(lambda part: lax.all_gather(part, axis), array)
    first = jax.tree.map(lambda part: part[0], everything)

    def turn(k, so_far):
        return combine(so_far, jax.tree.map(lambda part: part[k], everything))

    return lax.fori_loop(1, lax.axis_size(axis), turn, first)


def member_of(beam_index, half_index, halves):
    return beam_index % 2 + 2 * half_index + 2 * halves * (beam_index // 2)


def rms_round(values, gain):
    wide = values.astype(jnp.float32)
    mean_square = jnp.mean(wide * wide, axis=-1, keepdims=True)
    return (wide * lax.rsqrt(mean_square + EPSILON) * gain).astype(jnp.bfloat16)


def page_partial(queries, pages, key_pos, length, step_index):
    head_dim = queries.shape[-1]
    keys = pages[:, :, :head_dim]
    values = pages[:, :, head_dim:]
    scores = jnp.einsum(
        "jrhd,rkd->jrhk", queries, keys, preferred_element_type=jnp.float32
    ) * head_dim ** (-0.5)
    allowed = (key_pos < length[:, None]) & (key_pos > length[:, None] + step_index - WINDOW)
    scores = jnp.where(allowed[None, :, None, :], scores, NEGATIVE)
    highest = jnp.max(scores, axis=-1)
    weights = jnp.exp(scores - highest[..., None]).astype(jnp.bfloat16)
    totals = jnp.sum(weights.astype(jnp.float32), axis=-1)
    weighted = jnp.einsum("jrhk,rkd->jrhd", weights, values, preferred_element_type=jnp.float32)
    return (highest, totals, weighted)


def fresh_partial(queries, entries, count):
    head_dim = queries.shape[-1]
    keys = entries[..., :count, :head_dim]
    values = entries[..., :count, head_dim:]
    scores = jnp.einsum(
        "...hd,...kd->...hk", queries, keys, preferred_element_type=jnp.float32
    ) * head_dim ** (-0.5)
    highest = jnp.max(scores, axis=-1)
    weights = jnp.exp(scores - highest[..., None]).astype(jnp.bfloat16)
    totals = jnp.sum(weights.astype(jnp.float32), axis=-1)
    weighted = jnp.einsum("...hk,...kd->...hd", weights, values, preferred_element_type=jnp.float32)
    return (highest, totals, weighted)


def join_parts(first, second):
    highest = jnp.maximum(first[0], second[0])
    scale_first = jnp.exp(first[0] - highest)
    scale_second = jnp.exp(second[0] - highest)
    totals = first[1] * scale_first + second[1] * scale_second
    weighted = first[2] * scale_first[..., None] + second[2] * scale_second[..., None]
    return (highest, totals, weighted)


def feed_forward(mlp_in, w_gate, w_up, w_down):
    gate = jnp.dot(mlp_in, w_gate, preferred_element_type=jnp.float32)
    upward = jnp.dot(mlp_in, w_up, preferred_element_type=jnp.float32)
    hidden = (jax.nn.gelu(gate, approximate=True) * upward).astype(jnp.bfloat16)
    return jnp.dot(hidden, w_down, preferred_element_type=jnp.float32)


def rank_within(labels, offsets):
    earlier = (labels[None, :] == labels[:, None]) & (offsets[None, :] < offsets[:, None])
    return jnp.sum(earlier.astype(jnp.int32), axis=1)


def pick_half(array, halves, half):
    shaped = array.reshape((BEAMS // 2, halves, 2) + array.shape[1:])
    picked = lax.dynamic_index_in_dim(shaped, half, 1, keepdims=False)
    return picked.reshape((BEAMS,) + array.shape[1:])


def place_block(block, filler, halves, half):
    whole = jnp.full((BEAMS // 2, halves, 2) + block.shape[1:], filler, block.dtype)
    placed = lax.dynamic_update_slice_in_dim(
        whole, block.reshape((BEAMS // 2, 1, 2) + block.shape[1:]), half, 1
    )
    return placed.reshape((BEAMS * halves,) + block.shape[1:])


def on_device(
    x_steps,
    lengths,
    perm,
    parents,
    table,
    pool,
    norm_attn,
    w_query,
    w_keyval,
    w_out,
    norm_mlp,
    w_gate,
    w_up,
    w_down,
):
    steps, rows, width = x_steps.shape
    head_dim = pool.shape[2] // 2
    heads = w_query.shape[1] // head_dim
    span = table.shape[1] * pool.shape[1]
    req_count = lax.axis_size("req")
    kv_count = lax.axis_size("kv")
    group = lax.axis_index("req")
    member = lax.axis_index("kv")
    halves = kv_count // BEAMS
    half = member // 2 % halves
    beam = member % 2 + 2 * (member // (2 * halves))
    per_group = halves * rows
    group_rows = kv_count * rows
    quota = rows // req_count
    offsets = jnp.arange(rows, dtype=jnp.int32)
    slot_ids = group * per_group + half * rows + offsets
    placed = lax.dynamic_slice_in_dim(perm.reshape(req_count, per_group), half * rows, rows, 1)
    serving = lax.dynamic_index_in_dim(placed, group, 0, keepdims=False)
    target = jnp.sum(
        jnp.where(placed == slot_ids[None, :], jnp.arange(req_count, dtype=jnp.int32)[:, None], 0),
        axis=0,
    )
    anchor = serving // per_group
    send_order = jnp.argsort(target * rows + offsets)
    outgoing = x_steps[:, send_order].reshape(steps, req_count, quota, width)
    arrived = lax.all_to_all(outgoing, "req", split_axis=1, concat_axis=1, tiled=True).reshape(
        steps, rows, width
    )
    inputs = arrived[:, anchor * quota + rank_within(anchor, offsets)]
    length = lengths[serving]
    first_page = jnp.maximum(length - WINDOW + 1, 0) // PAGE
    key_pos = first_page[:, None] * PAGE + jnp.arange(span, dtype=jnp.int32)[None, :]
    device = group * kv_count + member
    pages = pool[table - device * pool.shape[0]].reshape(rows, span, 2 * head_dim)
    family = lax.dynamic_slice_in_dim(parents, group * group_rows, group_rows, 1)
    row_ids = jnp.arange(group_rows, dtype=jnp.int32)
    row_member = row_ids // rows
    row_half = row_member // 2 % halves
    within = row_ids % rows
    ancestor = row_member % 2 + 2 * (row_member // (2 * halves))
    recent = jnp.zeros((group_rows, steps, 2 * head_dim), jnp.bfloat16)
    results = []
    for step_index in range(steps):
        parent_rows = member_of(family[step_index], row_half, halves) * rows + within
        ancestor = ancestor[parent_rows]
        recent = recent[parent_rows]
        current = inputs[step_index]
        normed = rms_round(current, norm_attn)
        query = jnp.dot(normed, w_query, preferred_element_type=jnp.float32).astype(jnp.bfloat16)
        fresh = jnp.dot(normed, w_keyval, preferred_element_type=jnp.float32).astype(jnp.bfloat16)
        query_all, fresh_all = (
            lax.all_gather(query, "kv", axis=0, tiled=True),
            lax.all_gather(fresh, "kv", axis=0, tiled=True),
        )
        recent = recent.at[:, step_index].set(fresh_all)
        query_block = pick_half(query_all.reshape(kv_count, rows, heads, head_dim), halves, half)
        held = pick_half(ancestor.reshape(kv_count, rows), halves, half) == beam
        page = page_partial(query_block, pages, key_pos, length, step_index)
        held_heads = held[..., None]
        highest = place_block(jnp.where(held_heads, page[0], NEGATIVE), NEGATIVE, halves, half)
        totals = place_block(jnp.where(held_heads, page[1], 0.0), 0.0, halves, half)
        weighted = place_block(jnp.where(held_heads[..., None], page[2], 0.0), 0.0, halves, half)
        merged = merged_2((highest, totals, weighted), "kv", join_parts)
        page_own = tuple(
            (
                lax.dynamic_index_in_dim(member_part, member, 0, keepdims=False)
                for member_part in merged
            )
        )
        own_entries = lax.dynamic_slice_in_dim(recent, member * rows, rows, 0)
        joined = join_parts(
            page_own,
            fresh_partial(query.reshape(rows, heads, head_dim), own_entries, step_index + 1),
        )
        attended = (
            (joined[2] / joined[1][..., None]).astype(jnp.bfloat16).reshape(rows, heads * head_dim)
        )
        residual = (
            current.astype(jnp.float32)
            + jnp.dot(attended, w_out, preferred_element_type=jnp.float32)
        ).astype(jnp.bfloat16)
        terms = feed_forward(
            lax.all_gather(rms_round(residual, norm_mlp), "kv", axis=0, tiled=True),
            w_gate,
            w_up,
            w_down,
        )
        summed = lax.psum_scatter(
            terms.astype(jnp.bfloat16), "kv", scatter_dimension=0, tiled=True
        ).astype(jnp.float32)
        results.append((residual.astype(jnp.float32) + summed).astype(jnp.bfloat16))
    finished = jnp.stack(results)
    back_order = jnp.argsort(anchor * rows + offsets)
    leaving = finished[:, back_order].reshape(steps, req_count, quota, width)
    returned = lax.all_to_all(leaving, "req", split_axis=1, concat_axis=1, tiled=True).reshape(
        steps, rows, width
    )
    return returned[:, target * quota + rank_within(target, offsets)]


def solution(mesh):
    in_specs = (
        P(None, ("req", "kv"), None),
        P(),
        P(),
        P(),
        P(("req", "kv"), None),
        P(("req", "kv"), None, None),
        P(),
        P(),
        P(),
        P(),
        P(),
        P(None, "kv"),
        P(None, "kv"),
        P("kv", None),
    )
    out_specs = P(None, ("req", "kv"), None)
    return jax.shard_map(
        on_device, mesh=mesh, in_specs=in_specs, out_specs=out_specs, check_vma=False
    )
```

profile of v0, /device:TPU:1, one launch (start us, length us, event | category | flops | bytes accessed | tf_op | source)
XLA Modules:
  0.0 938.8 jit_solution(8522241222401222963)
XLA Ops:
  10.0 1.7 gather_fusion
  12.4 5.8 all-to-all-start
  27.0 7.8 gather_fusion.4
  35.8 3.2 convolution_convert_fusion.4
  39.0 20.2 %all_gather.90 = bf16[128,1536]{1,0:T(8,128)(2,1)S(1)} all-gather(bf16[8,1536]{1,0:T(8,128)(2,1)S(1)} %convolution_convert_fusion.4), channel_id=1, replica_groups=mesh['req'=8,'kv'=16] {'kv'}, dimensions={0}, use_global_device_ids=true | all-gather | bytes 417792 | tf_op jit(solution)/shard_map/all_gather | solution.py:165
  64.0 3.1 convolution_convert_fusion.7
  67.1 19.5 %all_gather.72 = bf16[128,1536]{1,0:T(8,128)(2,1)S(1)} all-gather(bf16[8,1536]{1,0:T(8,128)(2,1)S(1)} %convolution_convert_fusion.7), channel_id=1, replica_groups=mesh['req'=8,'kv'=16] {'kv'}, dimensions={0}, use_global_device_ids=true | all-gather | bytes 417792 | tf_op jit(solution)/shard_map/all_gather | solution.py:165
  86.7 2.8 bitcast_reduce_fusion.3
  93.2 3.1 convolution_convert_fusion.6
  96.3 17.8 %all_gather.78 = bf16[128,1536]{1,0:T(8,128)(2,1)S(1)} all-gather(bf16[8,1536]{1,0:T(8,128)(2,1)S(1)} %convolution_convert_fusion.6), channel_id=1, replica_groups=mesh['req'=8,'kv'=16] {'kv'}, dimensions={0}, use_global_device_ids=true | all-gather | bytes 417792 | tf_op jit(solution)/shard_map/all_gather | solution.py:165
  114.2 2.9 bitcast_reduce_fusion.2
  121.7 3.4 convert_reduce_fusion
  125.7 20.9 %all_gather.76 = bf16[128,256]{1,0:T(8,128)(2,1)S(1)} all-gather(bf16[8,256]{1,0:T(8,128)(2,1)S(1)} %convolution_convert_fusion.11), channel_id=1, replica_groups=mesh['req'=8,'kv'=16] {'kv'}, dimensions={0}, use_global_device_ids=true | all-gather | bytes 69632 | tf_op jit(solution)/shard_map/all_gather | solution.py:166
  149.5 16.4 %all_gather.82 = bf16[128,256]{1,0:T(8,128)(2,1)S(1)} all-gather(bf16[8,256]{1,0:T(8,128)(2,1)S(1)} %convolution_convert_fusion.10), channel_id=1, replica_groups=mesh['req'=8,'kv'=16] {'kv'}, dimensions={0}, use_global_device_ids=true | all-gather | bytes 69632 | tf_op jit(solution)/shard_map/all_gather | solution.py:166
  168.9 19.8 %all_gather.88 = bf16[128,256]{1,0:T(8,128)(2,1)S(1)} all-gather(bf16[8,256]{1,0:T(8,128)(2,1)S(1)} %convolution_convert_fusion.9), channel_id=1, replica_groups=mesh['req'=8,'kv'=16] {'kv'}, dimensions={0}, use_global_device_ids=true | all-gather | bytes 69632 | tf_op jit(solution)/shard_map/all_gather | solution.py:166
  191.6 16.4 %all_gather.94 = bf16[128,256]{1,0:T(8,128)(2,1)S(1)} all-gather(bf16[8,256]{1,0:T(8,128)(2,1)S(1)} %convolution_convert_fusion.8), channel_id=1, replica_groups=mesh['req'=8,'kv'=16] {'kv'}, dimensions={0}, use_global_device_ids=true | all-gather | bytes 69632 | tf_op jit(solution)/shard_map/all_gather | solution.py:166
  208.1 3.4 convert_reduce_fusion.3
  211.9 3.4 convert_reduce_fusion.2
  215.7 3.2 convolution_convert_fusion.5
  218.9 21.9 %all_gather.84 = bf16[128,1536]{1,0:T(8,128)(2,1)S(1)} all-gather(bf16[8,1536]{1,0:T(8,128)(2,1)S(1)} %convolution_convert_fusion.5), channel_id=1, replica_groups=mesh['req'=8,'kv'=16] {'kv'}, dimensions={0}, use_global_device_ids=true | all-gather | bytes 417792 | tf_op jit(solution)/shard_map/all_gather | solution.py:165
  240.9 2.7 bitcast_reduce_fusion.1
  243.6 2.1 copy-done.10
  248.8 20.0 %all_gather.91 = f32[16,16,8,12]{1,2,3,0:T(8,128)} all-gather(f32[1,16,8,12]{1,2,3,0:T(8,128)S(1)} %copy.375), channel_id=1, replica_groups=mesh['req'=8,'kv'=16] {'kv'}, dimensions={0}, use_global_device_ids=true | all-gather | bytes 104448 | tf_op jit(solution)/shard_map/all_gather | solution.py:14
  268.8 22.4 %all_gather.92 = f32[16,16,8,12]{1,2,3,0:T(8,128)} all-gather(f32[1,16,8,12]{1,2,3,0:T(8,128)S(1)} %copy.378), channel_id=1, replica_groups=mesh['req'=8,'kv'=16] {'kv'}, dimensions={0}, use_global_device_ids=true | all-gather | bytes 104448 | tf_op jit(solution)/shard_map/all_gather | solution.py:14
  291.2 20.8 %all_gather.73 = f32[16,16,8,12]{1,2,3,0:T(8,128)S(1)} all-gather(f32[1,16,8,12]{1,2,3,0:T(8,128)S(1)} %copy.320), channel_id=1, replica_groups=mesh['req'=8,'kv'=16] {'kv'}, dimensions={0}, use_global_device_ids=true | all-gather | bytes 104448 | tf_op jit(solution)/shard_map/all_gather | solution.py:14
  312.0 22.6 %all_gather.74 = f32[16,16,8,12]{1,2,3,0:T(8,128)S(1)} all-gather(f32[1,16,8,12]{1,2,3,0:T(8,128)S(1)} %copy.323), channel_id=1, replica_groups=mesh['req'=8,'kv'=16] {'kv'}, dimensions={0}, use_global_device_ids=true | all-gather | bytes 104448 | tf_op jit(solution)/shard_map/all_gather | solution.py:14
  334.6 21.6 %all_gather.79 = f32[16,16,8,12]{1,2,3,0:T(8,128)S(1)} all-gather(f32[1,16,8,12]{1,2,3,0:T(8,128)S(1)} %copy.341), channel_id=1, replica_groups=mesh['req'=8,'kv'=16] {'kv'}, dimensions={0}, use_global_device_ids=true | all-gather | bytes 104448 | tf_op jit(solution)/shard_map/all_gather | solution.py:14
  356.3 18.0 %all_gather.80 = f32[16,16,8,12]{1,2,3,0:T(8,128)S(1)} all-gather(f32[1,16,8,12]{1,2,3,0:T(8,128)S(1)} %copy.344), channel_id=1, replica_groups=mesh['req'=8,'kv'=16] {'kv'}, dimensions={0}, use_global_device_ids=true | all-gather | bytes 104448 | tf_op jit(solution)/shard_map/all_gather | solution.py:14
  374.3 19.4 %all_gather.85 = f32[16,16,8,12]{1,2,3,0:T(8,128)} all-gather(f32[1,16,8,12]{1,2,3,0:T(8,128)S(1)} %copy.358), channel_id=1, replica_groups=mesh['req'=8,'kv'=16] {'kv'}, dimensions={0}, use_global_device_ids=true | all-gather | bytes 104448 | tf_op jit(solution)/shard_map/all_gather | solution.py:14
  393.7 20.4 %all_gather.86 = f32[16,16,8,12]{1,2,3,0:T(8,128)} all-gather(f32[1,16,8,12]{1,2,3,0:T(8,128)S(1)} %copy.361), channel_id=1, replica_groups=mesh['req'=8,'kv'=16] {'kv'}, dimensions={0}, use_global_device_ids=true | all-gather | bytes 104448 | tf_op jit(solution)/shard_map/all_gather | solution.py:14
  420.4 2.7 fusion.37
  426.7 46.2 %while.83 = (s32[]{:T(128)}, f32[16,8,12]{0,1,2:T(8,128)S(1)}, f32[16,8,12]{0,1,2:T(8,128)S(1)}, f32[16,8,12,128]{3,2,1,0:T(8,128)S(1)}, f32[16,16,8,12]{1,2,3,0...) while((s32[]{:T(128)}, f32[16,8,12]{0,1,2:T(8,128)S(1)}, ...), condition=%wide.region_32.33_spmd, body=%wide.region_31.32_spmd.sunk | while | flops 599045 | bytes 4018327 | solution.py:20
  475.2 46.3 %while.80 = (s32[]{:T(128)}, f32[16,8,12]{0,1,2:T(8,128)S(1)}, f32[16,8,12]{0,1,2:T(8,128)S(1)}, f32[16,8,12,128]{3,2,1,0:T(8,128)S(1)}, f32[16,16,8,12]{1,2,3,0...) while((s32[]{:T(128)}, f32[16,8,12]{0,1,2:T(8,128)S(1)}, ...), condition=%wide.region_7.8_spmd, body=%wide.region_6.7_spmd.sunk | while | flops 599045 | bytes 4018327 | solution.py:20
  524.6 73.6 %while.81 = (s32[]{:T(128)}, f32[16,8,12]{0,1,2:T(8,128)S(1)}, f32[16,8,12]{0,1,2:T(8,128)S(1)}, f32[16,8,12,128]{3,2,1,0:T(8,128)}, f32[16,16,8,12]{1,2,3,0:T(8...) while((s32[]{:T(128)}, f32[16,8,12]{0,1,2:T(8,128)S(1)}, ...), condition=%wide.region_14.15_spmd, body=%wide.region_13.14_spmd.sunk | while | flops 599045 | bytes 4018327 | solution.py:20
  526.9 2.6 fusion.302
  531.8 2.6 fusion.302
  536.7 2.6 fusion.302
  541.7 2.6 fusion.302
  546.6 2.6 fusion.302
  551.5 2.6 fusion.302
  556.4 2.6 fusion.302
  561.3 2.6 fusion.302
  566.3 2.6 fusion.302
  571.2 2.6 fusion.302
  576.0 2.6 fusion.302
  580.9 2.6 fusion.302
  585.8 2.6 fusion.302
  590.7 2.6 fusion.302
  595.6 2.6 fusion.302
  601.4 3.4 multiply_reduce_fusion.3
  604.8 3.2 multiply_reduce_fusion.2
  610.3 46.2 %while.82 = (s32[]{:T(128)}, f32[16,8,12]{0,1,2:T(8,128)S(1)}, f32[16,8,12]{0,1,2:T(8,128)S(1)}, f32[16,8,12,128]{3,2,1,0:T(8,128)S(1)}, f32[16,16,8,12]{1,2,3,0...) while((s32[]{:T(128)}, f32[16,8,12]{0,1,2:T(8,128)S(1)}, ...), condition=%wide.region_23.24_spmd, body=%wide.region_22.23_spmd.sunk | while | flops 599045 | bytes 4018327 | solution.py:20
  657.8 3.2 multiply_reduce_fusion.1
  661.8 16.6 %all_gather.95 = bf16[128,1536]{1,0:T(8,128)(2,1)S(1)} all-gather(bf16[8,1536]{1,0:T(8,128)(2,1)S(1)} %get-tuple-element.991), channel_id=1, replica_groups=mesh['req'=8,'kv'=16] {'kv'}, dimensions={0}, use_global_device_ids=true | all-gather | bytes 417792 | tf_op jit(solution)/shard_map/all_gather | solution.py:196
  678.4 17.7 %all_gather.89 = bf16[128,1536]{1,0:T(8,128)(2,1)S(1)} all-gather(bf16[8,1536]{1,0:T(8,128)(2,1)S(1)} %get-tuple-element.990), channel_id=1, replica_groups=mesh['req'=8,'kv'=16] {'kv'}, dimensions={0}, use_global_device_ids=true | all-gather | bytes 417792 | tf_op jit(solution)/shard_map/all_gather | solution.py:196
  698.1 3.0 convolution_convert_fusion
  701.2 2.8 convolution_convert_fusion.1
  703.9 16.3 %all_gather.83 = bf16[128,1536]{1,0:T(8,128)(2,1)S(1)} all-gather(bf16[8,1536]{1,0:T(8,128)(2,1)} %get-tuple-element.989), channel_id=1, replica_groups=mesh['req'=8,'kv'=16] {'kv'}, dimensions={0}, use_global_device_ids=true | all-gather | bytes 417792 | tf_op jit(solution)/shard_map/all_gather | solution.py:196
  720.7 1.9 convolution_convert_fusion.2
  722.6 17.9 %all_gather.77 = bf16[128,1536]{1,0:T(8,128)(2,1)S(1)} all-gather(bf16[8,1536]{1,0:T(8,128)(2,1)S(1)} %copy-done.28), channel_id=1, replica_groups=mesh['req'=8,'kv'=16] {'kv'}, dimensions={0}, use_global_device_ids=true | all-gather | bytes 417792 | tf_op jit(solution)/shard_map/all_gather | solution.py:196
  740.9 1.9 convolution_convert_fusion.3
  744.1 170.9 %all-reduce.7.cloned.1.call-done = (bf16[128,1536]{1,0:T(8,128)(2,1)}, bf16[128,1536]{1,0:T(8,128)(2,1)}, bf16[128,1536]{1,0:T(8,128)(2,1)}, bf16[128,1536]{1,0:T(8,128)(2,1)}) async-done(((bf16[128,1536]{1,0:T(8,128)(2,1)}, bf16[128,1536]{1,0:T(8,128)(2,1)}, bf16[128,1536]{1,0:T(8,128)(2,1)}, bf16[128,1536]{1,0:T(8,128)(2,1)}), (bf16[128,1536]{1,0:T(8,128)(2,1)}, bf16[128,1536]{1,0:T(8,128)(2,1)}, ...) | async-done | bytes 1572880
  919.3 6.5 all-to-all-start.1
  925.8 5.0 all-to-all-done.1
  (596 shorter events, 243.4 us)
Async XLA Ops:
  6.5 691.6 %copy-start = (bf16[288,1536]{1,0:T(8,128)(2,1)S(1)}, bf16[288,1536]{1,0:T(8,128)(2,1)}, u32[]{:S(2)}) copy-start(bf16[288,1536]{1,0:T(8,128)(2,1)} %param.43) | copy-start | bytes 2654212
  7.4 27.4 %copy-start.38 = (s32[8]{0:T(128)}, s32[8]{0:T(128)S(1)}, u32[]{:S(2)}) copy-start(s32[8]{0:T(128)S(1)} %select_reduce_fusion) | copy-start | bytes 100
  12.4 22.5 %all-to-all-start = ((bf16[4,8,1,1536]{3,0,2,1:T(4,128)(2,1)}), bf16[4,8,1,1536]{3,0,2,1:T(4,128)(2,1)S(1)}, u32[]{:S(2)}, u32[]{:S(2)}) async-start(bf16[4,8,1,1536]{3,0,2,1:T(4,128)(2,1)} %copy.313), calls=%async_computation | async-start | bytes 196608 | tf_op jit(solution)/shard_map/all_to_all | solution.py:139
  18.2 407.1 %all-gather.11.cloned.1.call-start = ((), (), s32[]{:S(2)}) async-start(), calls=%async_computation.5 | async-start | bytes 13369344 | tf_op jit(solution)/shard_map/all_gather | solution.py:14
  27.0 8.8 copy-start.22
  35.6 23.7 %copy-start.6 = (bf16[72,128,256]{2,1,0:T(8,128)(2,1)S(1)}, bf16[72,128,256]{2,1,0:T(8,128)(2,1)}, u32[]{:S(2)}) copy-start(bf16[72,128,256]{2,1,0:T(8,128)(2,1)} %gather_fusion.4) | copy-start | bytes 14155780
  60.4 2.2 copy-start.9
  62.8 0.9 copy-start.13
  63.7 409.4 %all-gather.5.cloned.1.call-start = ((), (), s32[]{:S(2)}) async-start(), calls=%async_computation.2 | async-start | bytes 13369344 | tf_op jit(solution)/shard_map/all_gather | solution.py:14
  67.1 22.4 %slice-start.2 = ((s8[4718592]{0:T(1024)(128)(4,1)}), s8[4194304]{0:T(1024)(128)(4,1)S(1)}, s32[]{:S(2)}) async-start(s8[4718592]{0:T(1024)(128)(4,1)} %bitcast.579), calls=%async_computation.9 | async-start | bytes 8388608
  86.7 2.8 slice-start.3
  89.5 2.2 copy-start.7
  92.0 0.9 copy-start.14
  92.9 429.2 %all-gather.7.cloned.1.call-start = ((), (), s32[]{:S(2)}) async-start(), calls=%async_computation.3 | async-start | bytes 13369344 | tf_op jit(solution)/shard_map/all_gather | solution.py:14
  96.3 20.7 %slice-start.4 = ((s8[4718592]{0:T(1024)(128)(4,1)}), s8[4194304]{0:T(1024)(128)(4,1)S(1)}, s32[]{:S(2)}) async-start(s8[4718592]{0:T(1024)(128)(4,1)} %bitcast.582), calls=%async_computation.11 | async-start | bytes 8388608
  114.2 2.9 slice-start.5
  117.0 2.1 copy-start.8
  118.3 7.2 copy-start.5
  119.4 0.9 copy-start.15
  120.4 488.5 %all-gather.9.cloned.1.call-start = ((), (), s32[]{:S(2)}) async-start(), calls=%async_computation.4 | async-start | bytes 13369344 | tf_op jit(solution)/shard_map/all_gather | solution.py:14
  167.8 246.9 %copy-start.21 = (bf16[128,4,256]{2,1,0:T(4,128)(2,1)}, bf16[128,4,256]{2,1,0:T(4,128)(2,1)S(1)}, u32[]{:S(2)}) copy-start(bf16[128,4,256]{2,1,0:T(4,128)(2,1)S(1)} %scatter.15) | copy-start | bytes 786436
  190.5 226.4 %copy-start.20 = (bf16[128,4,256]{2,1,0:T(4,128)(2,1)}, bf16[128,4,256]{2,1,0:T(4,128)(2,1)S(1)}, u32[]{:S(2)}) copy-start(bf16[128,4,256]{2,1,0:T(4,128)(2,1)S(1)} %scatter.16) | copy-start | bytes 786436
  243.6 2.2 copy-start.10
  248.7 169.2 %copy-start.27 = (bf16[128,4,256]{2,1,0:T(4,128)(2,1)}, bf16[128,4,256]{2,1,0:T(4,128)(2,1)S(1)}, u32[]{:S(2)}) copy-start(bf16[128,4,256]{2,1,0:T(4,128)(2,1)S(1)} %scatter.19) | copy-start | bytes 786436
  248.8 171.7 %copy-start.11 = (f32[8,1152,8,12]{1,3,2,0:T(8,128)S(1)}, f32[8,1152,8,12]{1,3,2,0:T(8,128)}, u32[]{:S(2)}) copy-start(f32[8,1152,8,12]{1,3,2,0:T(8,128)} %copy-done.10) | copy-start | bytes 10616836
  312.0 107.6 %copy-start.18 = (f32[16,16,8,12]{1,2,3,0:T(8,128)}, f32[16,16,8,12]{1,2,3,0:T(8,128)S(1)}, u32[]{:S(2)}) copy-start(f32[16,16,8,12]{1,2,3,0:T(8,128)S(1)} %all_gather.73) | copy-start | bytes 294916
  334.6 85.0 %copy-start.19 = (f32[16,16,8,12]{1,2,3,0:T(8,128)}, f32[16,16,8,12]{1,2,3,0:T(8,128)S(1)}, u32[]{:S(2)}) copy-start(f32[16,16,8,12]{1,2,3,0:T(8,128)S(1)} %all_gather.74) | copy-start | bytes 294916
  356.3 62.5 %copy-start.16 = (f32[16,16,8,12]{1,2,3,0:T(8,128)}, f32[16,16,8,12]{1,2,3,0:T(8,128)S(1)}, u32[]{:S(2)}) copy-start(f32[16,16,8,12]{1,2,3,0:T(8,128)S(1)} %all_gather.79) | copy-start | bytes 294916
  374.3 45.3 %copy-start.17 = (f32[16,16,8,12]{1,2,3,0:T(8,128)}, f32[16,16,8,12]{1,2,3,0:T(8,128)S(1)}, u32[]{:S(2)}) copy-start(f32[16,16,8,12]{1,2,3,0:T(8,128)S(1)} %all_gather.80) | copy-start | bytes 294916
  414.8 0.6 copy-start.33
  414.8 8.3 copy-start.37
  415.6 1.4 copy-start.32
  417.1 7.6 copy-start.29
  423.5 0.9 copy-start.12
  424.4 490.5 %all-reduce.7.cloned.1.call-start = ((), (), s32[]{:S(2)}) async-start(), calls=%async_computation.6 | async-start | bytes 3145728
  472.8 1.0 copy-start.1
  475.2 46.6 %copy-start.40 = (f32[8,1,12]{2,1,0:T(1,128)S(1)}, f32[8,1,12]{2,1,0:T(1,128)}, u32[]{:S(2)}) copy-start(f32[8,1,12]{2,1,0:T(1,128)} %fusion.132) | copy-start | bytes 1156
  524.5 73.9 %copy-start.34 = (f32[8,12]{1,0:T(8,128)S(1)}, f32[8,12]{1,0:T(8,128)}, u32[]{:S(2)}) copy-start(f32[8,12]{1,0:T(8,128)} %copy-done.33) | copy-start | bytes 1156
  524.5 73.9 %copy-start.35 = (f32[8,12]{1,0:T(8,128)S(1)}, f32[8,12]{1,0:T(8,128)}, u32[]{:S(2)}) copy-start(f32[8,12]{1,0:T(8,128)} %convert_reduce_fusion.6) | copy-start | bytes 1156
  601.4 6.6 slice-start
  601.4 6.6 slice-start.1
  608.8 52.2 %copy-start.23 = (f32[8,1536]{1,0:T(8,128)}, f32[8,1536]{1,0:T(8,128)S(1)}, u32[]{:S(2)}) copy-start(f32[8,1536]{1,0:T(8,128)S(1)} %get-tuple-element.1037) | copy-start | bytes 147460
  610.2 46.5 %copy-start.30 = (f32[8,12]{1,0:T(8,128)S(1)}, f32[8,12]{1,0:T(8,128)}, u32[]{:S(2)}) copy-start(f32[8,12]{1,0:T(8,128)} %copy-done.29) | copy-start | bytes 1156
  610.2 46.5 %copy-start.31 = (f32[8,12]{1,0:T(8,128)S(1)}, f32[8,12]{1,0:T(8,128)}, u32[]{:S(2)}) copy-start(f32[8,12]{1,0:T(8,128)} %convert_reduce_fusion.5) | copy-start | bytes 1156
  656.4 4.6 copy-start.36
  656.7 39.3 %copy-start.2 = (bf16[1536,288]{0,1:T(8,128)(2,1)S(1)}, bf16[1536,288]{0,1:T(8,128)(2,1)}, u32[]{:S(2)}) copy-start(bf16[1536,288]{0,1:T(8,128)(2,1)} %param.41) | copy-start | bytes 2654212
  657.8 43.4 %copy-start.4 = (bf16[1536,288]{0,1:T(8,128)(2,1)S(1)}, bf16[1536,288]{0,1:T(8,128)(2,1)}, u32[]{:S(2)}) copy-start(bf16[1536,288]{0,1:T(8,128)(2,1)} %param.42) | copy-start | bytes 2654212
  661.0 17.3 %copy-start.25 = (f32[8,1536]{1,0:T(8,128)}, f32[8,1536]{1,0:T(8,128)S(1)}, u32[]{:S(2)}) copy-start(f32[8,1536]{1,0:T(8,128)S(1)} %get-tuple-element.1035) | copy-start | bytes 147460
  661.8 58.5 %copy-start.3 = (bf16[1536,288]{0,1:T(8,128)(2,1)S(1)}, bf16[1536,288]{0,1:T(8,128)(2,1)}, u32[]{:S(2)}) copy-start(bf16[1536,288]{0,1:T(8,128)(2,1)} %param.41) | copy-start | bytes 2654212
  701.2 21.4 %copy-start.28 = (bf16[8,1536]{1,0:T(8,128)(2,1)S(1)}, bf16[8,1536]{1,0:T(8,128)(2,1)}, u32[]{:S(2)}) copy-start(bf16[8,1536]{1,0:T(8,128)(2,1)} %get-tuple-element.988) | copy-start | bytes 73732
  720.7 22.1 %copy-start.43 = (u32[128]{0:T(128)S(1)}, u32[128]{0:T(128)}, u32[]{:S(2)}) copy-start(u32[128]{0:T(128)} %constant.568) | copy-start | bytes 1540
  720.7 23.3 %copy-start.41 = (s32[8]{0:T(128)S(1)}, s32[8]{0:T(128)}, u32[]{:S(2)}) copy-start(s32[8]{0:T(128)} %get-tuple-element.1040) | copy-start | bytes 100
  720.7 23.3 %copy-start.39 = (s32[8]{0:T(128)S(1)}, s32[8]{0:T(128)}, u32[]{:S(2)}) copy-start(s32[8]{0:T(128)} %copy-done.38) | copy-start | bytes 100
  720.7 23.3 %copy-start.42 = (s32[8]{0:T(128)S(1)}, s32[8]{0:T(128)}, u32[]{:S(2)}) copy-start(s32[8]{0:T(128)} %get-tuple-element.1038) | copy-start | bytes 100
  720.7 194.2 %copy-start.24 = (f32[8,1536]{1,0:T(8,128)S(1)}, f32[8,1536]{1,0:T(8,128)}, u32[]{:S(2)}) copy-start(f32[8,1536]{1,0:T(8,128)} %copy-done.23) | copy-start | bytes 147460
  720.7 195.0 %copy-start.26 = (f32[8,1536]{1,0:T(8,128)S(1)}, f32[8,1536]{1,0:T(8,128)}, u32[]{:S(2)}) copy-start(f32[8,1536]{1,0:T(8,128)} %copy-done.25) | copy-start | bytes 147460
  919.3 11.4 %all-to-all-start.1 = ((bf16[4,8,1,1536]{3,0,2,1:T(4,128)(2,1)}), bf16[4,8,1,1536]{3,0,2,1:T(4,128)(2,1)S(1)}, u32[]{:S(2)}, u32[]{:S(2)}) async-start(bf16[4,8,1,1536]{3,0,2,1:T(4,128)(2,1)} %bitcast.140), calls=%async_computation.1 | async-start | bytes 196608 | tf_op jit(solution)/shard_map/all_to_all | solution.py:208
Sparse Core Ops, SparseCore 0:
  63.8 97.4 all-gather.10
  163.5 91.9 all-gather.4
  257.7 102.1 all-gather.6
  424.5 152.7 all-gather.8
  742.9 172.0 all-reduce.6
where the time goes:
time: 955 us; the launch traced here: 939 us
  blocking collectives  387 us (41%)
  waiting for transfers between devices  176 us (18%)
  other arithmetic  146 us (15%)
  local copies, waits for them, and re-layouts  144 us (15%)
  matrix products  56.8 us (6%)
  between operations  15.5 us (2%)
  starting transfers between devices  12.6 us (1%)
    unnamed x6, waiting for transfers between devices  171 us
    all_gather x8, blocking collectives, merged_2(): everything = jax.tree.map(lambda part: lax.all_gather(part, axis), array)  165 us
    all_gather x4, blocking collectives, on_device(): lax.all_gather(query, 'kv', axis=0, tiled=True)  79.3 us
    all_gather x4, blocking collectives, on_device(): lax.all_gather(fresh, 'kv', axis=0, tiled=True)  73.6 us
    dynamic_slice x60, local copies, waits for them, and re-layouts, turn(): return combine(so_far, jax.tree.map(lambda part: part[k], everything))  71.7 us
    add x60, other arithmetic, join_parts(): first[2] * scale_first[..., None] + second[2] * scale_second[..., None]  70.3 us
    all_gather x4, blocking collectives, on_device(): lax.all_gather(rms_round(residual, norm_mlp), 'kv', axis=0, tiled=True)  68.5 us
    add x64, other arithmetic, join_parts(): totals = first[1] * scale_first + second[1] * scale_second  53.3 us
  transfers between devices with their start and end apart: 7, of which 2 were waited for; matrix products, arithmetic and copies ran while one was open for 27% of the time, Pallas kernels for 0%

commit v1 on v0

--- a/solution.py
+++ b/solution.py
@@ -1,3 +1,4 @@
+import functools
 import jax
 import jax.numpy as jnp
 from jax import lax
@@ -8,6 +9,37 @@
 BEAMS = 8
 EPSILON = 1e-06
 NEGATIVE = -1e30
+
+
+def _mix_turns(local_block, axis_no):
+    local_block = jnp.moveaxis(local_block, 0, axis_no)
+    later = local_block.shape
+    return local_block.reshape(
+        *later[:axis_no], later[axis_no] * later[axis_no + 1], *later[axis_no + 2 :]
+    )
+
+
+def run_the_targets(vals, axis_id, dim_no):
+    q_n = lax.axis_size(axis_id)
+    all_blocks = [(j, (j + 1) % q_n) for j in range(q_n)]
+    local_out, v_next = ([], [])
+    history = [(i, jj) for jj, i in all_blocks]
+    for b in range(q_n - 1):
+        if b % 2 == 0:
+            local_out.append(
+                lax.ppermute(local_out[-1] if local_out else vals, axis_id, all_blocks)
+            )
+        else:
+            v_next.append(lax.ppermute(v_next[-1] if v_next else vals, axis_id, history))
+    r_now = jnp.stack([*local_out[::-1], vals, *v_next], 0)
+    mid_arr = lax.axis_index(axis_id)
+    carry_in = len(local_out)
+    x_new = mid_arr - carry_in
+    r_now = r_now[(jnp.arange(q_n) - x_new) % q_n]
+    return _mix_turns(r_now, dim_no)
+
+
+sample_balance = functools.partial(run_the_targets, axis_id="kv", dim_no=0)
 
 
 def merged_2(array, axis, combine):
@@ -192,12 +224,7 @@
             current.astype(jnp.float32)
             + jnp.dot(attended, w_out, preferred_element_type=jnp.float32)
         ).astype(jnp.bfloat16)
-        terms = feed_forward(
-            lax.all_gather(rms_round(residual, norm_mlp), "kv", axis=0, tiled=True),
-            w_gate,
-            w_up,
-            w_down,
-        )
+        terms = feed_forward(sample_balance(rms_round(residual, norm_mlp)), w_gate, w_up, w_down)
         summed = lax.psum_scatter(
             terms.astype(jnp.bfloat16), "kv", scatter_dimension=0, tiled=True
         ).astype(jnp.float32)

time: 955 us -> 1050 us (1.099)
  starting transfers between devices: 12.6 us -> 87.7 us
  blocking collectives: 387 us -> 318 us
  local copies, waits for them, and re-layouts: 144 us -> 189 us
  waiting for transfers between devices: 176 us -> 219 us
    ppermute x0 -> x60, starting transfers between devices: none -> 75.1 us  [the longest x28 60.4 us: run_the_targets(): lax.ppermute(v_next[-1] if v_next else vals, axis_id, history)]
    all_gather x4 -> x0, blocking collectives: 68.5 us -> none  [on_device(): lax.all_gather(rms_round(residual, norm_mlp), 'kv', axis=0, tiled=True)]
    ppermute x0 -> x60, waiting for transfers between devices: none -> 44.1 us  [the longest x32 44 us: run_the_targets(): lax.ppermute(local_out[-1] if local_out else vals, axis_id, all_blocks)]
    unnamed x101 -> x233, local copies, waits for them, and re-layouts: 9.75 us -> 45.9 us
  transfers between devices with their start and end apart: 7 -> 67, of which waited for: 2 -> 16; matrix products, arithmetic and copies ran while one was open for 27% -> 30% of each run, Pallas kernels for 0% -> 0%
where the time goes in v1:
time: 1050 us; the launch traced here: 1030 us
  blocking collectives  318 us (30%)
  waiting for transfers between devices  219 us (21%)
  local copies, waits for them, and re-layouts  189 us (18%)
  other arithmetic  145 us (14%)
  starting transfers between devices  87.7 us (8%)
  matrix products  56.5 us (5%)
  between operations  16.2 us (2%)
    unnamed x6, waiting for transfers between devices  169 us
    all_gather x8, blocking collectives, merged_2(): everything = jax.tree.map(lambda part: lax.all_gather(part, axis), array)  165 us
    all_gather x4, blocking collectives, on_device(): lax.all_gather(query, 'kv', axis=0, tiled=True)  79.3 us
    all_gather x4, blocking collectives, on_device(): lax.all_gather(fresh, 'kv', axis=0, tiled=True)  73.8 us
    dynamic_slice x60, local copies, waits for them, and re-layouts, turn(): return combine(so_far, jax.tree.map(lambda part: part[k], everything))  71.7 us
    add x60, other arithmetic, join_parts(): first[2] * scale_first[..., None] + second[2] * scale_second[..., None]  69.9 us
    ppermute x28, starting transfers between devices, run_the_targets(): lax.ppermute(v_next[-1] if v_next else vals, axis_id, history)  60.4 us
    add x64, other arithmetic, join_parts(): totals = first[1] * scale_first + second[1] * scale_second  53.4 us
  transfers between devices with their start and end apart: 67, of which 16 were waited for; matrix products, arithmetic and copies ran while one was open for 30% of the time, Pallas kernels for 0%

profile of v1, /device:TPU:1, one launch (start us, length us, event | category | flops | bytes accessed | tf_op | source)
XLA Modules:
  0.0 1032.6 jit_solution(3752892807774124084)
XLA Ops:
  12.5 5.8 all-to-all-start
  27.1 7.8 gather_fusion.4
  36.0 3.2 convolution_convert_fusion.4
  39.2 20.2 %all_gather.75 = bf16[128,1536]{1,0:T(8,128)(2,1)S(1)} all-gather(bf16[8,1536]{1,0:T(8,128)(2,1)S(1)} %convolution_convert_fusion.4), channel_id=1, replica_groups=mesh['req'=8,'kv'=16] {'kv'}, dimensions={0}, use_global_device_ids=true | all-gather | bytes 417792 | tf_op jit(solution)/shard_map/all_gather | solution.py:197
  64.2 3.1 convolution_convert_fusion.7
  67.3 19.5 %all_gather.60 = bf16[128,1536]{1,0:T(8,128)(2,1)S(1)} all-gather(bf16[8,1536]{1,0:T(8,128)(2,1)S(1)} %convolution_convert_fusion.7), channel_id=1, replica_groups=mesh['req'=8,'kv'=16] {'kv'}, dimensions={0}, use_global_device_ids=true | all-gather | bytes 417792 | tf_op jit(solution)/shard_map/all_gather | solution.py:197
  86.9 2.8 bitcast_reduce_fusion.3
  93.3 3.1 convolution_convert_fusion.6
  96.4 17.5 %all_gather.65 = bf16[128,1536]{1,0:T(8,128)(2,1)S(1)} all-gather(bf16[8,1536]{1,0:T(8,128)(2,1)S(1)} %convolution_convert_fusion.6), channel_id=1, replica_groups=mesh['req'=8,'kv'=16] {'kv'}, dimensions={0}, use_global_device_ids=true | all-gather | bytes 417792 | tf_op jit(solution)/shard_map/all_gather | solution.py:197
  114.0 2.9 bitcast_reduce_fusion.2
  121.5 3.3 convert_reduce_fusion
  125.4 21.0 %all_gather.64 = bf16[128,256]{1,0:T(8,128)(2,1)S(1)} all-gather(bf16[8,256]{1,0:T(8,128)(2,1)S(1)} %convolution_convert_fusion.11), channel_id=1, replica_groups=mesh['req'=8,'kv'=16] {'kv'}, dimensions={0}, use_global_device_ids=true | all-gather | bytes 69632 | tf_op jit(solution)/shard_map/all_gather | solution.py:198
  149.3 16.8 %all_gather.69 = bf16[128,256]{1,0:T(8,128)(2,1)S(1)} all-gather(bf16[8,256]{1,0:T(8,128)(2,1)S(1)} %convolution_convert_fusion.10), channel_id=1, replica_groups=mesh['req'=8,'kv'=16] {'kv'}, dimensions={0}, use_global_device_ids=true | all-gather | bytes 69632 | tf_op jit(solution)/shard_map/all_gather | solution.py:198
  169.0 19.5 %all_gather.74 = bf16[128,256]{1,0:T(8,128)(2,1)S(1)} all-gather(bf16[8,256]{1,0:T(8,128)(2,1)S(1)} %convolution_convert_fusion.9), channel_id=1, replica_groups=mesh['req'=8,'kv'=16] {'kv'}, dimensions={0}, use_global_device_ids=true | all-gather | bytes 69632 | tf_op jit(solution)/shard_map/all_gather | solution.py:198
  191.5 16.5 %all_gather.79 = bf16[128,256]{1,0:T(8,128)(2,1)S(1)} all-gather(bf16[8,256]{1,0:T(8,128)(2,1)S(1)} %convolution_convert_fusion.8), channel_id=1, replica_groups=mesh['req'=8,'kv'=16] {'kv'}, dimensions={0}, use_global_device_ids=true | all-gather | bytes 69632 | tf_op jit(solution)/shard_map/all_gather | solution.py:198
  208.1 3.4 convert_reduce_fusion.3
  211.9 3.4 convert_reduce_fusion.2
  215.7 3.2 convolution_convert_fusion.5
  218.9 22.1 %all_gather.70 = bf16[128,1536]{1,0:T(8,128)(2,1)S(1)} all-gather(bf16[8,1536]{1,0:T(8,128)(2,1)S(1)} %convolution_convert_fusion.5), channel_id=1, replica_groups=mesh['req'=8,'kv'=16] {'kv'}, dimensions={0}, use_global_device_ids=true | all-gather | bytes 417792 | tf_op jit(solution)/shard_map/all_gather | solution.py:197
  241.0 2.7 bitcast_reduce_fusion.1
  248.9 19.9 %all_gather.76 = f32[16,16,8,12]{1,2,3,0:T(8,128)} all-gather(f32[1,16,8,12]{1,2,3,0:T(8,128)S(1)} %copy.375), channel_id=1, replica_groups=mesh['req'=8,'kv'=16] {'kv'}, dimensions={0}, use_global_device_ids=true | all-gather | bytes 104448 | tf_op jit(solution)/shard_map/all_gather | solution.py:46
  268.8 22.6 %all_gather.77 = f32[16,16,8,12]{1,2,3,0:T(8,128)} all-gather(f32[1,16,8,12]{1,2,3,0:T(8,128)S(1)} %copy.378), channel_id=1, replica_groups=mesh['req'=8,'kv'=16] {'kv'}, dimensions={0}, use_global_device_ids=true | all-gather | bytes 104448 | tf_op jit(solution)/shard_map/all_gather | solution.py:46
  291.4 20.6 %all_gather.61 = f32[16,16,8,12]{1,2,3,0:T(8,128)S(1)} all-gather(f32[1,16,8,12]{1,2,3,0:T(8,128)S(1)} %copy.320), channel_id=1, replica_groups=mesh['req'=8,'kv'=16] {'kv'}, dimensions={0}, use_global_device_ids=true | all-gather | bytes 104448 | tf_op jit(solution)/shard_map/all_gather | solution.py:46
  312.0 22.9 %all_gather.62 = f32[16,16,8,12]{1,2,3,0:T(8,128)S(1)} all-gather(f32[1,16,8,12]{1,2,3,0:T(8,128)S(1)} %copy.323), channel_id=1, replica_groups=mesh['req'=8,'kv'=16] {'kv'}, dimensions={0}, use_global_device_ids=true | all-gather | bytes 104448 | tf_op jit(solution)/shard_map/all_gather | solution.py:46
  334.9 21.5 %all_gather.66 = f32[16,16,8,12]{1,2,3,0:T(8,128)S(1)} all-gather(f32[1,16,8,12]{1,2,3,0:T(8,128)S(1)} %copy.341), channel_id=1, replica_groups=mesh['req'=8,'kv'=16] {'kv'}, dimensions={0}, use_global_device_ids=true | all-gather | bytes 104448 | tf_op jit(solution)/shard_map/all_gather | solution.py:46
  356.3 18.0 %all_gather.67 = f32[16,16,8,12]{1,2,3,0:T(8,128)S(1)} all-gather(f32[1,16,8,12]{1,2,3,0:T(8,128)S(1)} %copy.344), channel_id=1, replica_groups=mesh['req'=8,'kv'=16] {'kv'}, dimensions={0}, use_global_device_ids=true | all-gather | bytes 104448 | tf_op jit(solution)/shard_map/all_gather | solution.py:46
  374.3 19.6 %all_gather.71 = f32[16,16,8,12]{1,2,3,0:T(8,128)} all-gather(f32[1,16,8,12]{1,2,3,0:T(8,128)S(1)} %copy.358), channel_id=1, replica_groups=mesh['req'=8,'kv'=16] {'kv'}, dimensions={0}, use_global_device_ids=true | all-gather | bytes 104448 | tf_op jit(solution)/shard_map/all_gather | solution.py:46
  393.9 19.8 %all_gather.72 = f32[16,16,8,12]{1,2,3,0:T(8,128)} all-gather(f32[1,16,8,12]{1,2,3,0:T(8,128)S(1)} %copy.361), channel_id=1, replica_groups=mesh['req'=8,'kv'=16] {'kv'}, dimensions={0}, use_global_device_ids=true | all-gather | bytes 104448 | tf_op jit(solution)/shard_map/all_gather | solution.py:46
  420.0 2.7 fusion.37
  426.2 46.2 %while.83 = (s32[]{:T(128)}, f32[16,8,12]{0,1,2:T(8,128)S(1)}, f32[16,8,12]{0,1,2:T(8,128)S(1)}, f32[16,8,12,128]{3,2,1,0:T(8,128)S(1)}, f32[16,16,8,12]{1,2,3,0...) while((s32[]{:T(128)}, f32[16,8,12]{0,1,2:T(8,128)S(1)}, ...), condition=%wide.region_32.33_spmd, body=%wide.region_31.32_spmd.sunk | while | flops 599045 | bytes 4018327 | solution.py:52
  474.8 46.3 %while.80 = (s32[]{:T(128)}, f32[16,8,12]{0,1,2:T(8,128)S(1)}, f32[16,8,12]{0,1,2:T(8,128)S(1)}, f32[16,8,12,128]{3,2,1,0:T(8,128)S(1)}, f32[16,16,8,12]{1,2,3,0...) while((s32[]{:T(128)}, f32[16,8,12]{0,1,2:T(8,128)S(1)}, ...), condition=%wide.region_7.8_spmd, body=%wide.region_6.7_spmd.sunk | while | flops 599045 | bytes 4018327 | solution.py:52
  524.0 73.3 %while.81 = (s32[]{:T(128)}, f32[16,8,12]{0,1,2:T(8,128)S(1)}, f32[16,8,12]{0,1,2:T(8,128)S(1)}, f32[16,8,12,128]{3,2,1,0:T(8,128)}, f32[16,16,8,12]{1,2,3,0:T(8...) while((s32[]{:T(128)}, f32[16,8,12]{0,1,2:T(8,128)S(1)}, ...), condition=%wide.region_14.15_spmd, body=%wide.region_13.14_spmd.sunk | while | flops 599045 | bytes 4018327 | solution.py:52
  531.3 2.6 fusion.280
  600.6 3.4 multiply_reduce_fusion.3
  604.0 3.2 multiply_reduce_fusion.2
  609.4 46.2 %while.82 = (s32[]{:T(128)}, f32[16,8,12]{0,1,2:T(8,128)S(1)}, f32[16,8,12]{0,1,2:T(8,128)S(1)}, f32[16,8,12,128]{3,2,1,0:T(8,128)S(1)}, f32[16,16,8,12]{1,2,3,0...) while((s32[]{:T(128)}, f32[16,8,12]{0,1,2:T(8,128)S(1)}, ...), condition=%wide.region_23.24_spmd, body=%wide.region_22.23_spmd.sunk | while | flops 599045 | bytes 4018327 | solution.py:52
  656.9 3.3 multiply_reduce_fusion.1
  662.1 4.3 collective-permute-done.45
  666.7 5.7 collective-permute-done.46
  672.7 5.7 collective-permute-done.47
  678.7 5.7 collective-permute-done.48
  684.7 5.7 collective-permute-done.49
  690.7 5.7 collective-permute-done.50
  696.7 5.7 collective-permute-done.51
  702.4 5.1 collective-permute-start.53
  709.0 3.4 collective-permute-start.23
  714.6 3.7 collective-permute-done.37
  718.5 4.8 collective-permute-start.8
  725.0 3.4 collective-permute-start.24
  728.4 4.8 collective-permute-start.9
  734.9 3.4 collective-permute-start.25
  738.3 4.8 collective-permute-start.10
  744.7 3.4 collective-permute-start.26
  748.1 4.8 collective-permute-start.11
  754.6 3.4 collective-permute-start.27
  758.0 4.8 collective-permute-start.12
  764.7 3.4 collective-permute-start.28
  768.1 4.8 collective-permute-start.13
  775.2 4.7 collective-permute-start.44
  800.8 2.8 convolution_convert_fusion
  811.8 2.8 convolution_convert_fusion.1
  839.2 169.4 %all-reduce.7.cloned.1.call-done = (bf16[128,1536]{1,0:T(8,128)(2,1)}, bf16[128,1536]{1,0:T(8,128)(2,1)}, bf16[128,1536]{1,0:T(8,128)(2,1)}, bf16[128,1536]{1,0:T(8,128)(2,1)}) async-done(((bf16[128,1536]{1,0:T(8,128)(2,1)}, bf16[128,1536]{1,0:T(8,128)(2,1)}, bf16[128,1536]{1,0:T(8,128)(2,1)}, bf16[128,1536]{1,0:T(8,128)(2,1)}), (bf16[128,1536]{1,0:T(8,128)(2,1)}, bf16[128,1536]{1,0:T(8,128)(2,1)}, ...) | async-done | bytes 1572880
  1012.9 6.5 all-to-all-start.1
  1019.4 5.0 all-to-all-done.1
  (854 shorter events, 349.5 us)
Async XLA Ops:
  12.5 22.6 %all-to-all-start = ((bf16[4,8,1,1536]{3,0,2,1:T(4,128)(2,1)}), bf16[4,8,1,1536]{3,0,2,1:T(4,128)(2,1)S(1)}, u32[]{:S(2)}, u32[]{:S(2)}) async-start(bf16[4,8,1,1536]{3,0,2,1:T(4,128)(2,1)} %copy.313), calls=%async_computation | async-start | bytes 196608 | tf_op jit(solution)/shard_map/all_to_all | solution.py:171
  18.3 406.6 %all-gather.11.cloned.1.call-start = ((), (), s32[]{:S(2)}) async-start(), calls=%async_computation.5 | async-start | bytes 13369344 | tf_op jit(solution)/shard_map/all_gather | solution.py:46
  64.0 408.7 %all-gather.5.cloned.1.call-start = ((), (), s32[]{:S(2)}) async-start(), calls=%async_computation.2 | async-start | bytes 13369344 | tf_op jit(solution)/shard_map/all_gather | solution.py:46
  93.0 428.7 %all-gather.7.cloned.1.call-start = ((), (), s32[]{:S(2)}) async-start(), calls=%async_computation.3 | async-start | bytes 13369344 | tf_op jit(solution)/shard_map/all_gather | solution.py:46
  120.2 487.8 %all-gather.9.cloned.1.call-start = ((), (), s32[]{:S(2)}) async-start(), calls=%async_computation.4 | async-start | bytes 13369344 | tf_op jit(solution)/shard_map/all_gather | solution.py:46
  424.0 584.5 %all-reduce.7.cloned.1.call-start = ((), (), s32[]{:S(2)}) async-start(), calls=%async_computation.6 | async-start | bytes 3145728
  660.3 6.1 collective-permute-start.45
  660.7 6.0 collective-permute-start.30
  666.4 6.0 collective-permute-start.46
  666.7 6.0 collective-permute-start.31
  672.4 6.0 collective-permute-start.47
  672.7 6.0 collective-permute-start.32
  678.4 6.0 collective-permute-start.48
  678.7 6.0 collective-permute-start.33
  684.4 6.0 collective-permute-start.49
  684.7 6.0 collective-permute-start.34
  690.4 6.0 collective-permute-start.50
  690.7 6.0 collective-permute-start.35
  696.4 6.0 collective-permute-start.51
  696.7 12.2 %collective-permute-start.36 = (bf16[8,1536]{1,0:T(8,128)(2,1)S(1)}, bf16[8,1536]{1,0:T(8,128)(2,1)S(1)}, u32[]{:S(2)}, u32[]{:S(2)}) collective-permute-start(bf16[8,1536]{1,0:T(8,128)(2,1)S(1)} %collective-permute-done.35), channel_id=1, source_target_pairs={{0,1},{1,2},{2,3},{3,4},{4,5},{5,6},{6,7},{7,8},{8,9},{9,10},{10,1... | collective-permute-start | bytes 73736 | tf_op jit(solution)/shard_map/ppermute | solution.py:30
  702.4 10.0 collective-permute-start.52
  702.4 16.0 %collective-permute-start.53 = (bf16[8,1536]{1,0:T(8,128)(2,1)S(1)}, bf16[8,1536]{1,0:T(8,128)(2,1)S(1)}, u32[]{:S(2)}, u32[]{:S(2)}) collective-permute-start(bf16[8,1536]{1,0:T(8,128)(2,1)S(1)} %get-tuple-element.991), channel_id=1, source_target_pairs={{1,0},{2,1},{3,2},{4,3},{5,4},{6,5},{7,6},{8,7},{9,8},{10,9},{11,1... | collective-permute-start | bytes 73736 | tf_op jit(solution)/shard_map/ppermute | solution.py:33
  707.5 15.8 %collective-permute-start.38 = (bf16[8,1536]{1,0:T(8,128)(2,1)S(1)}, bf16[8,1536]{1,0:T(8,128)(2,1)S(1)}, u32[]{:S(2)}, u32[]{:S(2)}) collective-permute-start(bf16[8,1536]{1,0:T(8,128)(2,1)S(1)} %get-tuple-element.990), channel_id=1, source_target_pairs={{1,0},{2,1},{3,2},{4,3},{5,4},{6,5},{7,6},{8,7},{9,8},{10,9},{11,1... | collective-permute-start | bytes 73736 | tf_op jit(solution)/shard_map/ppermute | solution.py:33
  707.6 15.9 %collective-permute-start.15 = (bf16[8,1536]{1,0:T(8,128)(2,1)S(1)}, bf16[8,1536]{1,0:T(8,128)(2,1)S(1)}, u32[]{:S(2)}, u32[]{:S(2)}) collective-permute-start(bf16[8,1536]{1,0:T(8,128)(2,1)S(1)} %get-tuple-element.989), channel_id=1, source_target_pairs={{0,1},{1,2},{2,3},{3,4},{4,5},{5,6},{6,7},{7,8},{8,9},{9,10},{10,1... | collective-permute-start | bytes 73736 | tf_op jit(solution)/shard_map/ppermute | solution.py:30
  709.0 14.6 %collective-permute-start.23 = (bf16[8,1536]{1,0:T(8,128)(2,1)S(1)}, bf16[8,1536]{1,0:T(8,128)(2,1)S(1)}, u32[]{:S(2)}, u32[]{:S(2)}) collective-permute-start(bf16[8,1536]{1,0:T(8,128)(2,1)S(1)} %get-tuple-element.989), channel_id=1, source_target_pairs={{1,0},{2,1},{3,2},{4,3},{5,4},{6,5},{7,6},{8,7},{9,8},{10,9},{11,1... | collective-permute-start | bytes 73736 | tf_op jit(solution)/shard_map/ppermute | solution.py:33
  712.4 6.0 collective-permute-start.37
  718.4 6.6 collective-permute-start
  718.5 9.9 collective-permute-start.8
  723.3 5.1 collective-permute-start.54
  723.4 9.8 collective-permute-start.39
  723.5 9.7 collective-permute-start.16
  725.0 8.4 collective-permute-start.24
  728.4 6.4 collective-permute-start.1
  728.4 9.8 collective-permute-start.9
  733.3 9.8 collective-permute-start.40
  733.4 9.7 collective-permute-start.17
  734.9 8.4 collective-permute-start.25
  738.3 6.4 collective-permute-start.2
  738.3 9.8 collective-permute-start.10
  743.2 9.8 collective-permute-start.41
  743.3 9.7 collective-permute-start.18
  744.7 8.4 collective-permute-start.26
  748.1 6.4 collective-permute-start.3
  748.1 9.8 collective-permute-start.11
  753.0 9.8 collective-permute-start.42
  753.1 10.0 collective-permute-start.19
  754.6 8.7 collective-permute-start.27
  758.0 6.7 collective-permute-start.4
  758.0 10.1 collective-permute-start.12
  762.8 5.3 collective-permute-start.58
  763.1 9.8 collective-permute-start.43
  763.2 9.7 collective-permute-start.20
  764.7 10.5 %collective-permute-start.28 = (bf16[8,1536]{1,0:T(8,128)(2,1)S(1)}, bf16[8,1536]{1,0:T(8,128)(2,1)}, u32[]{:S(2)}, u32[]{:S(2)}) collective-permute-start(bf16[8,1536]{1,0:T(8,128)(2,1)S(1)} %collective-permute-done.27), channel_id=1, source_target_pairs={{1,0},{2,1},{3,2},{4,3},{5,4},{6,5},{7,6},{8,7},{9,8},{10,9},{11,1... | collective-permute-start | bytes 73736 | tf_op jit(solution)/shard_map/ppermute | solution.py:33
  768.1 6.3 collective-permute-start.5
  768.1 11.8 %collective-permute-start.13 = (bf16[8,1536]{1,0:T(8,128)(2,1)S(1)}, bf16[8,1536]{1,0:T(8,128)(2,1)}, u32[]{:S(2)}, u32[]{:S(2)}) collective-permute-start(bf16[8,1536]{1,0:T(8,128)(2,1)S(1)} %collective-permute-done.12), channel_id=1, source_target_pairs={{1,0},{2,1},{3,2},{4,3},{5,4},{6,5},{7,6},{8,7},{9,8},{10,9},{11,1... | collective-permute-start | bytes 73736 | tf_op jit(solution)/shard_map/ppermute | solution.py:33
  772.9 7.1 collective-permute-start.59
  773.0 7.1 collective-permute-start.21
  774.4 7.1 collective-permute-start.6
  775.2 8.5 collective-permute-start.44
  779.9 34.7 %collective-permute-start.29 = (bf16[8,1536]{1,0:T(8,128)(2,1)}, bf16[8,1536]{1,0:T(8,128)(2,1)}, u32[]{:S(2)}, u32[]{:S(2)}) collective-permute-start(bf16[8,1536]{1,0:T(8,128)(2,1)} %collective-permute-done.28), channel_id=1, source_target_pairs={{1,0},{2,1},{3,2},{4,3},{5,4},{6,5},{7,6},{8,7},{9,8},{10,9},{11,1... | collective-permute-start | bytes 73736 | tf_op jit(solution)/shard_map/ppermute | solution.py:33
  780.0 52.6 %collective-permute-start.14 = (bf16[8,1536]{1,0:T(8,128)(2,1)}, bf16[8,1536]{1,0:T(8,128)(2,1)}, u32[]{:S(2)}, u32[]{:S(2)}) collective-permute-start(bf16[8,1536]{1,0:T(8,128)(2,1)} %collective-permute-done.13), channel_id=1, source_target_pairs={{1,0},{2,1},{3,2},{4,3},{5,4},{6,5},{7,6},{8,7},{9,8},{10,9},{11,1... | collective-permute-start | bytes 73736 | tf_op jit(solution)/shard_map/ppermute | solution.py:33
  780.1 8.6 collective-permute-start.22
  781.5 36.4 %collective-permute-start.7 = (bf16[8,1536]{1,0:T(8,128)(2,1)}, bf16[8,1536]{1,0:T(8,128)(2,1)}, u32[]{:S(2)}, u32[]{:S(2)}) collective-permute-start(bf16[8,1536]{1,0:T(8,128)(2,1)} %collective-permute-done.6), channel_id=1, source_target_pairs={{0,1},{1,2},{2,3},{3,4},{4,5},{5,6},{6,7},{7,8},{8,9},{9,10},{10,1... | collective-permute-start | bytes 73736 | tf_op jit(solution)/shard_map/ppermute | solution.py:30
  1012.9 11.4 %all-to-all-start.1 = ((bf16[4,8,1,1536]{3,0,2,1:T(4,128)(2,1)}), bf16[4,8,1,1536]{3,0,2,1:T(4,128)(2,1)S(1)}, u32[]{:S(2)}, u32[]{:S(2)}) async-start(bf16[4,8,1,1536]{3,0,2,1:T(4,128)(2,1)} %bitcast.209), calls=%async_computation.1 | async-start | bytes 196608 | tf_op jit(solution)/shard_map/all_to_all | solution.py:235
  (89 other events, 4457.6 us)
Sparse Core Ops, SparseCore 0:
  64.1 97.4 all-gather.10
  163.7 91.9 all-gather.4
  258.0 102.0 all-gather.6
  424.1 153.2 all-gather.8
  838.0 170.5 all-reduce.6
